TPU v7x, 32 devices: a whole 2x2x4 slice. The times are simulated.
32 devices in a mesh: rows: 4 (over x, core), aux: 8 (over z, y).
Axes of the slice: x: 2, y: 2, z: 4, core: 2. Of those that a mesh axis runs over, the one named last changes fastest.
Arguments:
- b_rows: bfloat16 [6144, 8192], P(('rows', 'aux')), may hold values from -0.079589844 to 0.079589844
- pair_index: int32 [6144], P(('rows', 'aux')), may hold values from 0 to 6143, each once
- e_occ: float32 [512], replicated, may hold values from -3 to -0.5
- e_vir: float32 [1536], replicated, may hold values from 0.2 to 3
- occ_batch: int32 [1], replicated, may hold values from 0 to 127
- freq: float32 [1], replicated, may hold values from 0.3 to 3
Outputs:
- q_matrix: float32 [8192, 8192], P('aux', 'rows')
All inputs are finite; a program needn't handle non-finite values.
Results may differ from a plain program's by a relative error of at most 0.0022.
Values may be sent and summed in bfloat16 or wider, within the bound.
No kernel may reach another device: no remote copies, remote signals or barrier semaphores. Data moves between devices by JAX's collectives and lax.ppermute only.
A program may use at most 192 MiB of HBM per device.

v0:
```python
import jax
import jax.numpy as jnp
from jax import lax
from jax.sharding import PartitionSpec as P

NVIR = 1536
NOCC_B = 4


def row_weights(pairs, e_occ, e_vir, occ_batch, freq):
    batch_start = occ_batch[0] * NOCC_B
    e_batch = lax.dynamic_slice_in_dim(e_occ, batch_start, NOCC_B, 0)
    occ = pairs // NVIR
    vir = pairs % NVIR
    occ_hit = occ[:, None] == jnp.arange(NOCC_B, dtype=jnp.int32)[None, :]
    vir_hit = vir[:, None] == jnp.arange(e_vir.shape[0], dtype=jnp.int32)[None, :]
    e_low = jnp.sum(jnp.where(occ_hit, e_batch[None, :], 0.0), axis=1)
    e_high = jnp.sum(jnp.where(vir_hit, e_vir[None, :], 0.0), axis=1)
    delta = e_high - e_low
    return 2.0 * delta / (delta * delta + freq[0] * freq[0])


def contract(left, right):
    return lax.dot_general(
        left, right, (((0,), (0,)), ((), ())), preferred_element_type=jnp.float32
    )


def body(b_rows, pair_index, e_occ, e_vir, occ_batch, freq):
    group_pairs = lax.all_gather(pair_index, "aux", axis=0, tiled=True)
    regrouped = lax.all_to_all(b_rows, "aux", split_axis=1, concat_axis=0, tiled=True)
    weight = row_weights(group_pairs, e_occ, e_vir, occ_batch, freq)
    scaled = (weight[:, None] * regrouped.astype(jnp.float32)).astype(jnp.bfloat16)
    partial_value = contract(scaled, lax.all_gather(regrouped, "aux", axis=1, tiled=True))
    return lax.psum_scatter(partial_value, "rows", scatter_dimension=1, tiled=True)


def solution(mesh):
    placed = (P(("rows", "aux"), None), P(("rows", "aux")), P(), P(), P(), P())
    return jax.shard_map(
        body, mesh=mesh, in_specs=placed, out_specs=P("aux", "rows"), check_vma=False
    )
```

profile of v0, /device:TPU:0, one launch (start us, length us, event | category | flops | bytes accessed | tf_op | source)
XLA Modules:
  0.0 842.8 jit_solution(14496598981891353015)
XLA Ops:
  6.5 0.0 copy-start.2
  6.5 0.0 copy-start
  6.5 0.0 copy-start.1
  6.5 0.0 all-gather.2.cloned.1.call-start
  6.5 2.4 copy.12
  8.9 77.9 %all_to_all.19 = bf16[192,8,1024]{2,0,1:T(8,128)(2,1)} all-to-all(bf16[192,8,1024]{2,0,1:T(8,128)(2,1)S(1)} %bitcast.13), channel_id=1, replica_groups=mesh['rows'=4,'aux'=8] {'aux'}, dimensions={1} | all-to-all | bytes 6291456 | tf_op jit(solution)/shard_map/all_to_all | solution.py:31
  86.8 0.0 all-gather.2.cloned.1.call-update
  86.8 0.0 reduce-scatter.2.cloned.1.call-start
  88.2 0.0 copy-done.2
  88.2 0.6 dynamic-slice
  89.4 0.8 dynamic_slice.3
  90.2 0.0 copy-done
  90.2 0.2 dynamic-update-slice
  90.4 42.0 %all-reduce = s32[1536]{0:T(1024)S(1)} all-reduce(s32[1536]{0:T(1024)S(1)} %dynamic-update-slice), channel_id=1, replica_groups=mesh['rows'=4,'aux'=8] {'aux'}, use_global_device_ids=true, to_apply=%add | all-reduce | flops 1536 | bytes 12288
  132.4 0.1 select_reduce_fusion.1
  132.5 0.0 copy-done.1
  132.5 1.3 select_reduce_fusion
  133.8 432.7 %all-gather.2.cloned.1.call-done = bf16[1536,8192]{1,0:T(8,128)(2,1)} async-done(((bf16[1536,1024]{1,0:T(8,128)(2,1)}), bf16[1536,8192]{1,0:T(8,128)(2,1)}) %all-gather.2.cloned.1.call-update) | async-done | bytes 25165840 | tf_op jit(solution)/shard_map/all_gather | solution.py:34
  566.5 34.5 %fusion = f32[1024,8192]{1,0:T(8,128)} fusion(bf16[1536,8192]{1,0:T(8,128)(2,1)} %all-gather.2.cloned.1.call-done, bf16[1536,1024]{1,0:T(8,128)(2,1)} %bitcast.12, f32[1536]{0:T(1024)S(1)} %add_divide_fusion), kind=kOutput, calls=%fused_computation.3 | convolution fusion | flops 25774522368 | bytes 61872128 | tf_op jit(solution)/shard_map/dot_general | solution.py:24
  601.0 0.0 reduce-scatter.2.cloned.1.call-update
  601.0 234.9 %reduce-scatter.2.cloned.1.call-done = f32[1024,2048]{1,0:T(8,128)} async-done(((f32[1024,8192]{1,0:T(8,128)}), f32[1024,2048]{1,0:T(8,128)}) %reduce-scatter.2.cloned.1.call-update) | async-done | bytes 8388624 | tf_op jit(solution)/shard_map/reduce_scatter | solution.py:35
  (3 shorter events, 0.0 us)
Async XLA Ops:
  6.5 81.6 %copy-start.2 = (u32[32]{0:T(128)S(1)}, u32[32]{0:T(128)}, u32[]{:S(2)}) copy-start(u32[32]{0:T(128)} %constant.32) | copy-start | bytes 388
  6.5 83.7 %copy-start = (s32[192]{0:T(256)S(1)}, s32[192]{0:T(256)}, u32[]{:S(2)}) copy-start(s32[192]{0:T(256)} %param.7) | copy-start | bytes 2308
  6.5 126.0 %copy-start.1 = (f32[1536]{0:T(1024)S(1)}, f32[1536]{0:T(1024)}, u32[]{:S(2)}) copy-start(f32[1536]{0:T(1024)} %param.9) | copy-start | bytes 18436
  6.5 560.0 %all-gather.2.cloned.1.call-start = ((), (), s32[]{:S(2)}) async-start(), calls=%async_computation.2 | async-start | bytes 28311552 | tf_op jit(solution)/shard_map/all_gather | solution.py:34
  86.8 749.1 %reduce-scatter.2.cloned.1.call-start = ((), (), s32[]{:S(2)}) async-start(), calls=%async_computation.3 | async-start | bytes 41943040 | tf_op jit(solution)/shard_map/reduce_scatter | solution.py:35
Sparse Core Ops, SparseCore 0:
  86.9 479.5 all-gather.1
  601.2 234.7 reduce-scatter.1
where the time goes:
time: 843 us
  waiting for transfers between devices  668 us (79%)
  blocking collectives  120 us (14%)
  matrix products  34.5 us (4%)
  between operations  15.4 us (2%)
    all_gather x1, waiting for transfers between devices, body(): lax.all_gather(regrouped, 'aux', axis=1, tiled=True)  433 us
    reduce_scatter x1, waiting for transfers between devices, body(): lax.psum_scatter(partial_value, 'rows', scatter_dimension=1, tiled=True)  235 us
    all_to_all x1, blocking collectives, body(): lax.all_to_all(b_rows, 'aux', split_axis=1, concat_axis=0, tiled=True)  77.9 us
    unnamed x1, blocking collectives  42 us
    dot_general x1, matrix products, contract(): lax.dot_general(left, right, (((0,), (0,)), ((), ())), preferred_element_...  34.5 us
  transfers between devices with their start and end apart: 2, of which 2 were waited for; matrix products, arithmetic and copies ran while one was open for 0% of the time, Pallas kernels for 0%

commit v1 on v0

--- a/solution.py
+++ b/solution.py
@@ -5,6 +5,28 @@
 
 NVIR = 1536
 NOCC_B = 4
+
+
+def joined_along(tiles, dim):
+    dims = list(tiles.shape[1:])
+    dims[dim] *= tiles.shape[0]
+    return jnp.moveaxis(tiles, 0, dim).reshape(dims)
+
+
+def gather_around(value, axis, dim):
+    devices = lax.axis_size(axis)
+    pairs = [(i, (i + 1) % devices) for i in range(devices)]
+    back = [(b, a) for a, b in pairs]
+    lower, upper = ([], [])
+    for step in range(devices - 1):
+        if step % 2 == 0:
+            lower.append(lax.ppermute(lower[-1] if lower else value, axis, pairs))
+        else:
+            upper.append(lax.ppermute(upper[-1] if upper else value, axis, back))
+    pieces = jnp.stack([*lower[::-1], value, *upper])
+    shift = lax.axis_index(axis) - len(lower)
+    pieces = pieces[(jnp.arange(devices) - shift) % devices]
+    return joined_along(pieces, dim)
 
 
 def row_weights(pairs, e_occ, e_vir, occ_batch, freq):
@@ -31,7 +53,7 @@
     regrouped = lax.all_to_all(b_rows, "aux", split_axis=1, concat_axis=0, tiled=True)
     weight = row_weights(group_pairs, e_occ, e_vir, occ_batch, freq)
     scaled = (weight[:, None] * regrouped.astype(jnp.float32)).astype(jnp.bfloat16)
-    partial_value = contract(scaled, lax.all_gather(regrouped, "aux", axis=1, tiled=True))
+    partial_value = contract(scaled, gather_around(regrouped, "aux", 1))
     return lax.psum_scatter(partial_value, "rows", scatter_dimension=1, tiled=True)
 
 

time: 843 us -> 942 us (1.12)
  waiting for transfers between devices: 668 us -> 556 us
  starting transfers between devices: 0.04 us -> 81.8 us
  local copies, waits for them, and re-layouts: 3.93 us -> 77.9 us
  blocking collectives: 120 us -> 148 us
  other arithmetic: 1.45 us -> 28.5 us
    all_gather x1 -> x0, waiting for transfers between devices: 433 us -> none  [body(): lax.all_gather(regrouped, 'aux', axis=1, tiled=True)]
    ppermute x0 -> x7, waiting for transfers between devices: none -> 321 us  [the longest x4 265 us: gather_around(): lower.append(lax.ppermute(lower[-1] if lower else value, axis, pairs))]
    ppermute x0 -> x7, starting transfers between devices: none -> 81.8 us  [the longest x3 75.3 us: gather_around(): upper.append(lax.ppermute(upper[-1] if upper else value, axis, back))]
    transpose x0 -> x1, local copies, waits for them, and re-layouts: none -> 32.8 us  [joined_along(): return jnp.moveaxis(tiles, 0, dim).reshape(dims)]
    gather x0 -> x3, local copies, waits for them, and re-layouts: none -> 31 us  [gather_around(): pieces = pieces[(jnp.arange(devices) - shift) % devices]]
    unnamed x1, blocking collectives: 42 us -> 69.8 us
    transpose x0 -> x1, other arithmetic: none -> 24.8 us  [joined_along(): return jnp.moveaxis(tiles, 0, dim).reshape(dims)]
    unnamed x9 -> x26, local copies, waits for them, and re-layouts: 0.82 us -> 10.6 us
  transfers between devices with their start and end apart: 2 -> 8, of which waited for: 2 -> 5; matrix products, arithmetic and copies ran while one was open for 0% -> 2% of each run, Pallas kernels for 0% -> 0%
where the time goes in v1:
time: 942 us; the launch traced here: 940 us
  waiting for transfers between devices  556 us (59%)
  blocking collectives  148 us (16%)
  starting transfers between devices  81.8 us (9%)
  local copies, waits for them, and re-layouts  77.9 us (8%)
  matrix products  32.9 us (3%)
  other arithmetic  28.5 us (3%)
  between operations  15.5 us (2%)
    ppermute x4, waiting for transfers between devices, gather_around(): lower.append(lax.ppermute(lower[-1] if lower else value, axis, pairs))  265 us
    reduce_scatter x1, waiting for transfers between devices, body(): lax.psum_scatter(partial_value, 'rows', scatter_dimension=1, tiled=True)  236 us
    all_to_all x1, blocking collectives, body(): lax.all_to_all(b_rows, 'aux', split_axis=1, concat_axis=0, tiled=True)  77.8 us
    ppermute x3, starting transfers between devices, gather_around(): upper.append(lax.ppermute(upper[-1] if upper else value, axis, back))  75.3 us
    unnamed x1, blocking collectives  69.8 us
    ppermute x3, waiting for transfers between devices, gather_around(): upper.append(lax.ppermute(upper[-1] if upper else value, axis, back))  55.5 us
    dot_general x1, matrix products, contract(): lax.dot_general(left, right, (((0,), (0,)), ((), ())), preferred_element_...  32.9 us
    transpose x1, local copies, waits for them, and re-layouts, joined_along(): return jnp.moveaxis(tiles, 0, dim).reshape(dims)  32.8 us
  transfers between devices with their start and end apart: 8, of which 5 were waited for; matrix products, arithmetic and copies ran while one was open for 2% of the time, Pallas kernels for 0%

profile of v1, /device:TPU:0, one launch (start us, length us, event | category | flops | bytes accessed | tf_op | source)
XLA Modules:
  0.0 940.3 jit_solution(16573942885105325422)
XLA Ops:
  6.5 0.0 copy-start.7
  6.5 0.0 copy-start.5
  6.5 0.0 copy-start.6
  6.5 0.0 reduce-scatter.2.cloned.1.call-start
  6.5 2.4 copy.19
  8.9 77.8 %all_to_all.19 = bf16[192,8,1024]{2,0,1:T(8,128)(2,1)S(1)} all-to-all(bf16[192,8,1024]{2,0,1:T(8,128)(2,1)S(1)} %bitcast.39), channel_id=1, replica_groups=mesh['rows'=4,'aux'=8] {'aux'}, dimensions={1} | all-to-all | bytes 6291456 | tf_op jit(solution)/shard_map/all_to_all | solution.py:53
  86.7 1.5 collective-permute-start
  88.2 69.9 %collective-permute-done = bf16[1536,1024]{1,0:T(8,128)(2,1)S(1)} collective-permute-done((bf16[1536,1024]{1,0:T(8,128)(2,1)S(1)}, bf16[1536,1024]{1,0:T(8,128)(2,1)S(1)}, u32[]{:S(2)}, u32[]{:S(2)}) %collective-permute-start) | collective-permute-done | bytes 3145760 | tf_op jit(solution)/shard_map/ppermute | solution.py:23
  158.1 0.0 copy-start
  158.1 0.0 collective-permute-start.1
  158.1 4.7 collective-permute-start.4
  162.8 128.3 %collective-permute-done.1 = bf16[1536,1024]{1,0:T(8,128)(2,1)S(1)} collective-permute-done((bf16[1536,1024]{1,0:T(8,128)(2,1)S(1)}, bf16[1536,1024]{1,0:T(8,128)(2,1)S(1)}, u32[]{:S(2)}, u32[]{:S(2)}) %collective-permute-start.1) | collective-permute-done | bytes 3145760 | tf_op jit(solution)/shard_map/ppermute | solution.py:23
  291.1 0.0 copy-start.2
  291.1 2.5 collective-permute-start.2
  293.6 0.0 collective-permute-done.4
  293.6 0.0 copy-done
  293.6 67.6 %collective-permute-start.5 = (bf16[1536,1024]{1,0:T(8,128)(2,1)}, bf16[1536,1024]{1,0:T(8,128)(2,1)}, u32[]{:S(2)}, u32[]{:S(2)}) collective-permute-start(bf16[1536,1024]{1,0:T(8,128)(2,1)} %collective-permute-done.4), channel_id=1, source_target_pairs={{1,0},{2,1},{3,2},{4,3},{5,4},{6,5},{7,6},{0,7},{9,8},{10,9},{11,1... | collective-permute-start | bytes 9437192 | tf_op jit(solution)/shard_map/ppermute | solution.py:25
  361.2 0.0 copy-done.2
  361.2 66.8 %collective-permute-done.2 = bf16[1536,1024]{1,0:T(8,128)(2,1)} collective-permute-done((bf16[1536,1024]{1,0:T(8,128)(2,1)S(1)}, bf16[1536,1024]{1,0:T(8,128)(2,1)}, u32[]{:S(2)}, u32[]{:S(2)}) %collective-permute-start.2) | collective-permute-done | bytes 3145760 | tf_op jit(solution)/shard_map/ppermute | solution.py:23
  428.1 2.6 collective-permute-start.3
  432.0 0.8 dynamic_slice.3
  432.7 0.0 copy-done.7
  432.7 0.6 dynamic-slice
  434.0 0.0 copy-done.5
  434.0 0.3 dynamic-update-slice
  434.3 69.8 %all-reduce = s32[1536]{0:T(1024)S(1)} all-reduce(s32[1536]{0:T(1024)S(1)} %dynamic-update-slice), channel_id=1, replica_groups=mesh['rows'=4,'aux'=8] {'aux'}, use_global_device_ids=true, to_apply=%add | all-reduce | flops 1536 | bytes 12288
  504.1 0.1 select_reduce_fusion.1
  504.2 0.0 copy-done.6
  504.2 1.3 select_reduce_fusion
  505.5 0.1 div.18
  505.6 0.0 copy-start.3
  505.6 0.0 copy-start.1
  505.6 2.2 multiply_convert_fusion
  507.9 0.0 collective-permute-done.5
  507.9 2.9 collective-permute-start.6
  510.8 0.0 collective-permute-done.3
  510.8 2.2 bitcast_dynamic-update-slice_fusion.6
  513.0 2.2 bitcast_dynamic-update-slice_fusion.5
  515.2 0.0 copy-done.3
  515.2 0.3 bitcast_dynamic-update-slice_fusion.4
  515.5 0.0 copy-done.1
  515.5 0.3 bitcast_dynamic-update-slice_fusion.3
  515.9 0.3 constant_dynamic-update-slice_fusion
  516.2 2.2 bitcast_dynamic-update-slice_fusion.2
  518.4 2.2 bitcast_dynamic-update-slice_fusion.1
  520.6 55.5 %collective-permute-done.6 = bf16[1536,1024]{1,0:T(8,128)(2,1)S(1)} collective-permute-done((bf16[1536,1024]{1,0:T(8,128)(2,1)}, bf16[1536,1024]{1,0:T(8,128)(2,1)S(1)}, u32[]{:S(2)}, u32[]{:S(2)}) %collective-permute-start.6) | collective-permute-done | bytes 3145760 | tf_op jit(solution)/shard_map/ppermute | solution.py:25
  576.1 0.3 bitcast_dynamic-update-slice_fusion
  576.4 9.0 fusion.3
  585.4 11.0 %gather_fusion = bf16[8,768,1024]{2,1,0:T(8,128)(2,1)} fusion(bf16[8,768,1024]{2,1,0:T(8,128)(2,1)} %get-tuple-element.5, s32[1024]{0:T(1024)S(1)} %pad_clamp_fusion), kind=kCustom, calls=%fused_computation | custom fusion | bytes 25165856 | tf_op jit(solution)/shard_map/gather | solution.py:28
  596.4 10.9 %gather_fusion.1 = bf16[8,768,1024]{2,1,0:T(8,128)(2,1)} fusion(bf16[8,768,1024]{2,1,0:T(8,128)(2,1)} %get-tuple-element.6, s32[1024]{0:T(1024)S(1)} %pad_clamp_fusion), kind=kCustom, calls=%fused_computation.1 | custom fusion | bytes 25165856 | tf_op jit(solution)/shard_map/gather | solution.py:28
  607.3 24.8 %maximum_bitcast_fusion = bf16[1536,8,1024]{2,0,1:T(8,128)(2,1)} fusion(bf16[8,768,1024]{2,1,0:T(8,128)(2,1)} %gather_fusion.1, bf16[8,768,1024]{2,1,0:T(8,128)(2,1)} %gather_fusion), kind=kLoop, calls=%fused_computation.2 | loop fusion | flops 50331648 | bytes 50331648 | tf_op jit(solution)/shard_map/transpose | solution.py:13
  632.1 0.0 copy-start.4
  632.1 32.8 %copy.16 = bf16[1536,8,1024]{0,2,1:T(8,128)(2,1)} copy(bf16[1536,8,1024]{2,0,1:T(8,128)(2,1)} %maximum_bitcast_fusion) | data formatting | bytes 50331648 | tf_op jit(solution)/shard_map/transpose | solution.py:13
  665.0 0.0 copy-done.4
  665.0 32.9 %fusion.4 = f32[1024,8192]{1,0:T(8,128)} fusion(bf16[1536,1024]{1,0:T(8,128)(2,1)S(1)} %bitcast.41, bf16[1536,8192]{0,1:T(8,128)(2,1)} %bitcast.38), kind=kOutput, calls=%fused_computation.31 | convolution fusion | flops 25769803776 | bytes 61865984 | tf_op jit(solution)/shard_map/dot_general | solution.py:46
  697.9 0.0 reduce-scatter.2.cloned.1.call-update
  697.9 235.6 %reduce-scatter.2.cloned.1.call-done = f32[1024,2048]{1,0:T(8,128)} async-done(((f32[1024,8192]{1,0:T(8,128)}), f32[1024,2048]{1,0:T(8,128)}) %reduce-scatter.2.cloned.1.call-update) | async-done | bytes 8388624 | tf_op jit(solution)/shard_map/reduce_scatter | solution.py:57
  (5 shorter events, 0.1 us)
Async XLA Ops:
  6.5 426.2 %copy-start.7 = (u32[32]{0:T(128)S(1)}, u32[32]{0:T(128)}, u32[]{:S(2)}) copy-start(u32[32]{0:T(128)} %constant.54) | copy-start | bytes 388
  6.5 427.4 %copy-start.5 = (s32[192]{0:T(256)S(1)}, s32[192]{0:T(256)}, u32[]{:S(2)}) copy-start(s32[192]{0:T(256)} %param.7) | copy-start | bytes 2308
  6.5 497.6 %copy-start.6 = (f32[1536]{0:T(1024)S(1)}, f32[1536]{0:T(1024)}, u32[]{:S(2)}) copy-start(f32[1536]{0:T(1024)} %param.9) | copy-start | bytes 18436
  6.5 926.9 %reduce-scatter.2.cloned.1.call-start = ((), (), s32[]{:S(2)}) async-start(), calls=%async_computation.2 | async-start | bytes 41943040 | tf_op jit(solution)/shard_map/reduce_scatter | solution.py:57
  86.7 71.4 %collective-permute-start = (bf16[1536,1024]{1,0:T(8,128)(2,1)S(1)}, bf16[1536,1024]{1,0:T(8,128)(2,1)S(1)}, u32[]{:S(2)}, u32[]{:S(2)}) collective-permute-start(bf16[1536,1024]{1,0:T(8,128)(2,1)S(1)} %bitcast.35), channel_id=1, source_target_pairs={{0,1},{1,2},{2,3},{3,4},{4,5},{5,6},{6,7},{7,0},{8,9},{9,10},{10,1... | collective-permute-start | bytes 9437192 | tf_op jit(solution)/shard_map/ppermute | solution.py:23
  158.1 135.5 %copy-start = (bf16[1536,1024]{1,0:T(8,128)(2,1)}, bf16[1536,1024]{1,0:T(8,128)(2,1)S(1)}, u32[]{:S(2)}) copy-start(bf16[1536,1024]{1,0:T(8,128)(2,1)S(1)} %collective-permute-done) | copy-start | bytes 9437188
  158.1 133.0 %collective-permute-start.1 = (bf16[1536,1024]{1,0:T(8,128)(2,1)S(1)}, bf16[1536,1024]{1,0:T(8,128)(2,1)S(1)}, u32[]{:S(2)}, u32[]{:S(2)}) collective-permute-start(bf16[1536,1024]{1,0:T(8,128)(2,1)S(1)} %collective-permute-done), channel_id=1, source_target_pairs={{0,1},{1,2},{2,3},{3,4},{4,5},{5,6},{6,7},{7,0},{8,9},{9,10},{10,1... | collective-permute-start | bytes 9437192 | tf_op jit(solution)/shard_map/ppermute | solution.py:23
  158.1 135.5 %collective-permute-start.4 = (bf16[1536,1024]{1,0:T(8,128)(2,1)S(1)}, bf16[1536,1024]{1,0:T(8,128)(2,1)}, u32[]{:S(2)}, u32[]{:S(2)}) collective-permute-start(bf16[1536,1024]{1,0:T(8,128)(2,1)S(1)} %bitcast.36), channel_id=1, source_target_pairs={{1,0},{2,1},{3,2},{4,3},{5,4},{6,5},{7,6},{0,7},{9,8},{10,9},{11,1... | collective-permute-start | bytes 9437192 | tf_op jit(solution)/shard_map/ppermute | solution.py:25
  291.1 70.1 %copy-start.2 = (bf16[1536,1024]{1,0:T(8,128)(2,1)}, bf16[1536,1024]{1,0:T(8,128)(2,1)S(1)}, u32[]{:S(2)}) copy-start(bf16[1536,1024]{1,0:T(8,128)(2,1)S(1)} %collective-permute-done.1) | copy-start | bytes 9437188
  291.1 137.0 %collective-permute-start.2 = (bf16[1536,1024]{1,0:T(8,128)(2,1)S(1)}, bf16[1536,1024]{1,0:T(8,128)(2,1)}, u32[]{:S(2)}, u32[]{:S(2)}) collective-permute-start(bf16[1536,1024]{1,0:T(8,128)(2,1)S(1)} %collective-permute-done.1), channel_id=1, source_target_pairs={{0,1},{1,2},{2,3},{3,4},{4,5},{5,6},{6,7},{7,0},{8,9},{9,10},{10,1... | collective-permute-start | bytes 9437192 | tf_op jit(solution)/shard_map/ppermute | solution.py:23
  293.6 214.3 %collective-permute-start.5 = (bf16[1536,1024]{1,0:T(8,128)(2,1)}, bf16[1536,1024]{1,0:T(8,128)(2,1)}, u32[]{:S(2)}, u32[]{:S(2)}) collective-permute-start(bf16[1536,1024]{1,0:T(8,128)(2,1)} %collective-permute-done.4), channel_id=1, source_target_pairs={{1,0},{2,1},{3,2},{4,3},{5,4},{6,5},{7,6},{0,7},{9,8},{10,9},{11,1... | collective-permute-start | bytes 9437192 | tf_op jit(solution)/shard_map/ppermute | solution.py:25
  428.1 82.7 %collective-permute-start.3 = (bf16[1536,1024]{1,0:T(8,128)(2,1)}, bf16[1536,1024]{1,0:T(8,128)(2,1)}, u32[]{:S(2)}, u32[]{:S(2)}) collective-permute-start(bf16[1536,1024]{1,0:T(8,128)(2,1)} %collective-permute-done.2), channel_id=1, source_target_pairs={{0,1},{1,2},{2,3},{3,4},{4,5},{5,6},{6,7},{7,0},{8,9},{9,10},{10,1... | collective-permute-start | bytes 9437192 | tf_op jit(solution)/shard_map/ppermute | solution.py:23
  505.6 9.6 %copy-start.3 = (bf16[1536,1024]{1,0:T(8,128)(2,1)S(1)}, bf16[1536,1024]{1,0:T(8,128)(2,1)}, u32[]{:S(2)}) copy-start(bf16[1536,1024]{1,0:T(8,128)(2,1)} %copy-done.2) | copy-start | bytes 9437188
  505.6 9.9 %copy-start.1 = (bf16[1536,1024]{1,0:T(8,128)(2,1)S(1)}, bf16[1536,1024]{1,0:T(8,128)(2,1)}, u32[]{:S(2)}) copy-start(bf16[1536,1024]{1,0:T(8,128)(2,1)} %copy-done) | copy-start | bytes 9437188
  507.9 68.2 %collective-permute-start.6 = (bf16[1536,1024]{1,0:T(8,128)(2,1)}, bf16[1536,1024]{1,0:T(8,128)(2,1)S(1)}, u32[]{:S(2)}, u32[]{:S(2)}) collective-permute-start(bf16[1536,1024]{1,0:T(8,128)(2,1)} %collective-permute-done.5), channel_id=1, source_target_pairs={{1,0},{2,1},{3,2},{4,3},{5,4},{6,5},{7,6},{0,7},{9,8},{10,9},{11,1... | collective-permute-start | bytes 9437192 | tf_op jit(solution)/shard_map/ppermute | solution.py:25
  632.1 32.8 %copy-start.4 = (bf16[8,192,1024]{2,1,0:T(8,128)(2,1)S(1)}, bf16[8,192,1024]{2,1,0:T(8,128)(2,1)}, u32[]{:S(2)}) copy-start(bf16[8,192,1024]{2,1,0:T(8,128)(2,1)} %multiply_convert_fusion) | copy-start | bytes 9437188
Sparse Core Ops, SparseCore 0:
  698.0 235.4 reduce-scatter.1
